TPU v7x, 512 devices: a whole 4x4x16 slice. The times are simulated.
512 devices in a mesh: men: 32 (over z_lo, y, core), women: 16 (over z_hi, x).
Axes of the slice: x: 4, y: 4, z: 16 (z_hi: 4, z_lo: 4; z = z_hi * 4 + z_lo), core: 2. Of those that a mesh axis runs over, the one named last changes fastest.
Arguments:
- men_embed: bfloat16 [65536, 128], P(('men', 'women')), may hold values from -4 to 4
- women_embed: bfloat16 [16384, 128], P(('women', 'men')), may hold values from -4 to 4
- men_count: int32 [65536], P('men'), may hold values from 1 to 297, as said below
- women_count: int32 [16384], P('women'), may hold values from 1 to 299
- women_root: float32 [16384], P('women'), may hold values from 0.5 to 6, as said below
- men_cotangent: float32 [65536], P('men'), may hold values from -300 to 300
- women_cotangent: float32 [16384], P('women'), may hold values from 24 to 864, as said below
Outputs:
- men_grad: float32 [65536, 128], P(('men', 'women'))
- women_grad: float32 [16384, 128], P(('women', 'men'))
Inputs may be any that keep to these rules, and one draw needn't show every extreme that they name: `men_count`: integer masses of the male types. `women_root`: positive. `women_cotangent`: positive.
All inputs are finite; a program needn't handle non-finite values.
Results may differ from a plain program's by a relative error of at most 0.0031.
Values may be sent and summed in bfloat16 or wider, within the bound.
No kernel may reach another device: no remote copies, remote signals or barrier semaphores. Data moves between devices by JAX's collectives and lax.ppermute only.
A program may use at most 64 MiB of HBM per device.

v0:
```python
import jax
import jax.numpy as jnp
from jax import lax
from jax.sharding import PartitionSpec as P


def kernel_tile(men_rows, women_block):
    surplus = lax.dot_general(
        men_rows, women_block, (((1,), (1,)), ((), ())), preferred_element_type=jnp.float32
    )
    return jnp.exp(0.5 * surplus)


def body(
    men_embed, women_embed, men_count, women_count, women_root, men_cotangent, women_cotangent
):
    men_rows = lax.all_gather(men_embed, "women", axis=0, tiled=True)
    women_rows = lax.all_gather(women_embed, "men", axis=0, tiled=True)
    men_mass = men_count.astype(jnp.float32)
    women_mass = women_count.astype(jnp.float32)
    stored = kernel_tile(men_rows, women_rows)

    def sweep(work):
        return work(stored, women_rows, 0)

    def first_work(kernel, women_block, col_start):
        weighted = kernel * women_root[None, :]
        product = jnp.dot(
            weighted.astype(jnp.bfloat16), women_block, preferred_element_type=jnp.float32
        )
        return ((jnp.sum(weighted, axis=1), product), ())

    row_partial, weighted_v = sweep(first_work)[0]
    row_mass = lax.psum(row_partial, "women")
    men_disc = jnp.sqrt(row_mass * row_mass + 4.0 * men_mass)
    men_root = 2.0 * men_mass / (row_mass + men_disc)

    def second_work(kernel, women_block, col_start):
        return ((), (jnp.sum(kernel * men_root[:, None], axis=0),))

    col_partial = sweep(second_work)[1][0]
    col_mass = lax.psum(col_partial, "men")
    women_disc = jnp.sqrt(col_mass * col_mass + 4.0 * women_mass)
    col_grad = -women_cotangent / women_disc

    def third_work(kernel, women_block, col_start):
        weighted = kernel * col_grad[None, :]
        product = jnp.dot(
            weighted.astype(jnp.bfloat16), women_block, preferred_element_type=jnp.float32
        )
        return ((jnp.sum(weighted, axis=1), product), ())

    row_back, direct_v = sweep(third_work)[0]
    row_cot = lax.psum(row_back, "women")
    row_grad = -(men_cotangent + men_root * row_cot) / men_disc
    men_term = 0.5 * (row_grad[:, None] * weighted_v + men_root[:, None] * direct_v)
    men_grad = lax.psum_scatter(men_term, "women", scatter_dimension=0, tiled=True)

    def fourth_work(kernel, women_block, col_start):
        tangent = (
            0.5
            * kernel
            * (row_grad[:, None] * women_root[None, :] + men_root[:, None] * col_grad[None, :])
        ).astype(jnp.bfloat16)
        return (
            (),
            (
                lax.dot_general(
                    tangent, men_rows, (((0,), (0,)), ((), ())), preferred_element_type=jnp.float32
                ),
            ),
        )

    women_terms = sweep(fourth_work)[1][0]
    women_grad = lax.psum_scatter(women_terms, "men", scatter_dimension=0, tiled=True)
    return (men_grad, women_grad)


def solution(mesh):
    return jax.shard_map(
        body,
        mesh=mesh,
        in_specs=(
            P(("men", "women"), None),
            P(("women", "men"), None),
            P("men"),
            P("women"),
            P("women"),
            P("men"),
            P("women"),
        ),
        out_specs=(P(("men", "women"), None), P(("women", "men"), None)),
        check_vma=False,
    )
```

profile of v0, /device:TPU:8, one launch (start us, length us, event | category | flops | bytes accessed | tf_op | source)
XLA Modules:
  0.0 561.4 jit_solution(11899115688756769913)
XLA Ops:
  7.2 0.0 copy-start.1
  7.2 0.0 reduce-scatter.5.cloned.1.call-start
  7.2 44.3 %all_gather.7 = bf16[1024,128]{1,0:T(8,128)(2,1)S(1)} all-gather(bf16[32,128]{1,0:T(8,128)(2,1)} %param.8), channel_id=1, replica_groups=mesh['men'=32,'women'=16] {'men'}, dimensions={0}, use_global_device_ids=true | all-gather | bytes 270336 | tf_op jit(solution)/shard_map/all_gather | solution.py:18
  51.5 58.4 %all_gather.6 = bf16[2048,128]{1,0:T(8,128)(2,1)S(1)} all-gather(bf16[128,128]{1,0:T(8,128)(2,1)} %param.7), channel_id=1, replica_groups=mesh['men'=32,'women'=16] {'women'}, dimensions={0}, use_global_device_ids=true | all-gather | bytes 557056 | tf_op jit(solution)/shard_map/all_gather | solution.py:17
  109.9 0.0 copy-start.3
  109.9 0.0 copy-start.4
  109.9 4.8 multiply_reduce_fusion.2
  114.7 46.7 %psum.21 = f32[2048]{0:T(1024)S(1)} all-reduce(f32[2048]{0:T(1024)S(1)} %get-tuple-element.2), channel_id=1, replica_groups=mesh['men'=32,'women'=16] {'women'}, use_global_device_ids=true, to_apply=%region_1.0 | all-reduce | flops 2048 | bytes 16384 | tf_op jit(solution)/shard_map/psum | solution.py:34
  161.5 0.0 copy-done.1
  161.5 0.0 copy-start.2
  161.5 0.0 copy-start
  161.5 4.0 multiply_reduce_fusion
  165.5 64.6 %psum.22 = f32[1024]{0:T(1024)S(1)} all-reduce(f32[1024]{0:T(1024)S(1)} %multiply_reduce_fusion), channel_id=1, replica_groups=mesh['men'=32,'women'=16] {'men'}, use_global_device_ids=true, to_apply=%region_3.0 | all-reduce | flops 1024 | bytes 8192 | tf_op jit(solution)/shard_map/psum | solution.py:42
  230.2 0.0 copy-done.3
  230.2 0.0 copy-done.4
  230.2 4.0 multiply_reduce_fusion.1
  234.2 48.8 %psum.23 = f32[2048]{0:T(1024)S(1)} all-reduce(f32[2048]{0:T(1024)S(1)} %multiply_reduce_fusion.1), channel_id=1, replica_groups=mesh['men'=32,'women'=16] {'women'}, use_global_device_ids=true, to_apply=%region_5.0 | all-reduce | flops 2048 | bytes 16384 | tf_op jit(solution)/shard_map/psum | solution.py:54
  283.0 0.0 copy-done.2
  283.0 0.0 copy-done
  283.0 5.9 %fusion.4 = f32[1024,128]{1,0:T(8,128)} fusion(bf16[2048,128]{1,0:T(8,128)(2,1)S(1)} %all_gather.6, f32[2048,1024]{0,1:T(8,128)} %get-tuple-element.3, f32[2048]{0:T(1024)S(1)} %negate_divide_fusion, f32[1024]{0:T(1024)S(1)} %rsqrt_multiply_fusion, f32[2048]{0:T(1024)S(1)} %add_divide_fusion, f32[1024]{0:T(1024)S(1)} %copy-done), kind=kOutput, calls=%fused_computation.11 | convolution fusion | flops 549453824 | bytes 9461760 | tf_op jit(solution)/shard_map/dot_general | solution.py:68
  288.9 0.0 reduce-scatter.5.cloned.1.call-update
  289.0 0.0 reduce-scatter.3.cloned.1.call-start
  289.0 5.0 fusion.5
  294.0 6.1 %fusion.8 = f32[2048,128]{1,0:T(8,128)} fusion(f32[2048,128]{1,0:T(8,128)S(1)} %fusion.5, bf16[1024,128]{1,0:T(8,128)(2,1)S(1)} %all_gather.7, f32[2048,1024]{0,1:T(8,128)} %get-tuple-element.3, f32[1024]{0:T(1024)S(1)} %copy-done, f32[2048]{0:T(1024)S(1)} %negate_divide_fusion), kind=kOutput, calls=%fused_computation.15 | convolution fusion | flops 541851648 | bytes 10760192 | tf_op jit(solution)/shard_map/dot_general | solution.py:28
  300.1 0.0 reduce-scatter.3.cloned.1.call-update
  300.1 132.9 %reduce-scatter.5.cloned.1.call-done = f32[32,128]{1,0:T(8,128)} async-done(((f32[1024,128]{1,0:T(8,128)}), f32[32,128]{1,0:T(8,128)}) %reduce-scatter.5.cloned.1.call-update) | async-done | bytes 16400 | tf_op jit(solution)/shard_map/reduce_scatter | solution.py:75
  432.9 121.7 %reduce-scatter.3.cloned.1.call-done = f32[128,128]{1,0:T(8,128)} async-done(((f32[2048,128]{1,0:T(8,128)}), f32[128,128]{1,0:T(8,128)}) %reduce-scatter.3.cloned.1.call-update) | async-done | bytes 65552 | tf_op jit(solution)/shard_map/reduce_scatter | solution.py:57
  (3 shorter events, 0.0 us)
Async XLA Ops:
  7.2 154.3 %copy-start.1 = (s32[2048]{0:T(1024)S(1)}, s32[2048]{0:T(1024)}, u32[]{:S(2)}) copy-start(s32[2048]{0:T(1024)} %param.9) | copy-start | bytes 24580
  7.2 425.8 %reduce-scatter.5.cloned.1.call-start = ((), (), s32[]{:S(2)}) async-start(), calls=%async_computation.3 | async-start | bytes 540672 | tf_op jit(solution)/shard_map/reduce_scatter | solution.py:75
  109.9 120.3 %copy-start.3 = (s32[1024]{0:T(1024)S(1)}, s32[1024]{0:T(1024)}, u32[]{:S(2)}) copy-start(s32[1024]{0:T(1024)} %param.10) | copy-start | bytes 12292
  109.9 120.3 %copy-start.4 = (f32[1024]{0:T(1024)S(1)}, f32[1024]{0:T(1024)}, u32[]{:S(2)}) copy-start(f32[1024]{0:T(1024)} %param.13) | copy-start | bytes 12292
  161.5 121.5 %copy-start.2 = (f32[2048]{0:T(1024)S(1)}, f32[2048]{0:T(1024)}, u32[]{:S(2)}) copy-start(f32[2048]{0:T(1024)} %param.12) | copy-start | bytes 24580
  161.5 121.5 %copy-start = (f32[1024]{0:T(1024)S(1)}, f32[1024]{0:T(1024)}, u32[]{:S(2)}) copy-start(f32[1024]{0:T(1024)} %param.11) | copy-start | bytes 12292
  289.0 265.6 %reduce-scatter.3.cloned.1.call-start = ((), (), s32[]{:S(2)}) async-start(), calls=%async_computation.2 | async-start | bytes 1114112 | tf_op jit(solution)/shard_map/reduce_scatter | solution.py:57
Sparse Core Ops, SparseCore 0:
  289.1 143.8 reduce-scatter.4
  437.6 116.9 reduce-scatter.2
where the time goes:
time: 562 us; the launch traced here: 561 us
  blocking collectives  263 us (47%)
  waiting for transfers between devices  255 us (45%)
  matrix products  21.8 us (4%)
  between operations  14.1 us (3%)
  other arithmetic  8.05 us (1%)
    reduce_scatter x1, waiting for transfers between devices, body(): lax.psum_scatter(women_terms, 'men', scatter_dimension=0, tiled=True)  133 us
    reduce_scatter x1, waiting for transfers between devices, body(): lax.psum_scatter(men_term, 'women', scatter_dimension=0, tiled=True)  122 us
    psum x1, blocking collectives, body(): col_mass = lax.psum(col_partial, 'men')  64.6 us
    all_gather x1, blocking collectives, body(): men_rows = lax.all_gather(men_embed, 'women', axis=0, tiled=True)  58.4 us
    psum x1, blocking collectives, body(): row_cot = lax.psum(row_back, 'women')  48.8 us
    psum x1, blocking collectives, body(): row_mass = lax.psum(row_partial, 'women')  46.7 us
    all_gather x1, blocking collectives, body(): women_rows = lax.all_gather(women_embed, 'men', axis=0, tiled=True)  44.3 us
  transfers between devices with their start and end apart: 2, of which 2 were waited for; matrix products, arithmetic and copies ran while one was open for 2% of the time, Pallas kernels for 0%

commit v1 on v0

--- a/solution.py
+++ b/solution.py
@@ -14,7 +14,9 @@
 def body(
     men_embed, women_embed, men_count, women_count, women_root, men_cotangent, women_cotangent
 ):
-    men_rows = lax.all_gather(men_embed, "women", axis=0, tiled=True)
+    men_rows = jnp.concatenate(
+        lax.all_to_all(jnp.stack([men_embed] * lax.axis_size("women")), "women", 0, 0), axis=0
+    )
     women_rows = lax.all_gather(women_embed, "men", axis=0, tiled=True)
     men_mass = men_count.astype(jnp.float32)
     women_mass = women_count.astype(jnp.float32)

time: 562 us -> 538 us (0.957)
  blocking collectives: 263 us -> 218 us
  starting transfers between devices: 0.08 us -> 17.7 us
    all_gather x1 -> x0, blocking collectives: 58.4 us -> none  [body(): men_rows = lax.all_gather(men_embed, 'women', axis=0, tiled=True)]
    all_to_all x0 -> x1, starting transfers between devices: none -> 17.7 us  [body(): lax.all_to_all(jnp.stack([men_embed] * lax.axis_size('women')), 'women',...]
    psum x1, blocking collectives: 46.7 us -> 61.4 us  [body(): row_mass = lax.psum(row_partial, 'women')]
  transfers between devices with their start and end apart: 2 -> 3, of which waited for: 2 -> 2; matrix products, arithmetic and copies ran while one was open for 2% -> 2% of each run, Pallas kernels for 0% -> 0%
where the time goes in v1:
time: 538 us; the launch traced here: 537 us
  waiting for transfers between devices  256 us (48%)
  blocking collectives  218 us (41%)
  matrix products  21.8 us (4%)
  starting transfers between devices  17.7 us (3%)
  between operations  14.2 us (3%)
  other arithmetic  8.05 us (1%)
    reduce_scatter x1, waiting for transfers between devices, body(): lax.psum_scatter(women_terms, 'men', scatter_dimension=0, tiled=True)  135 us
    reduce_scatter x1, waiting for transfers between devices, body(): lax.psum_scatter(men_term, 'women', scatter_dimension=0, tiled=True)  122 us
    psum x1, blocking collectives, body(): row_mass = lax.psum(row_partial, 'women')  61.4 us
    psum x1, blocking collectives, body(): col_mass = lax.psum(col_partial, 'men')  60.7 us
    all_gather x1, blocking collectives, body(): women_rows = lax.all_gather(women_embed, 'men', axis=0, tiled=True)  48.7 us
    psum x1, blocking collectives, body(): row_cot = lax.psum(row_back, 'women')  46.8 us
    all_to_all x1, starting transfers between devices, body(): lax.all_to_all(jnp.stack([men_embed] * lax.axis_size('women')), 'women',...  17.7 us
  transfers between devices with their start and end apart: 3, of which 2 were waited for; matrix products, arithmetic and copies ran while one was open for 2% of the time, Pallas kernels for 0%

profile of v1, /device:TPU:8, one launch (start us, length us, event | category | flops | bytes accessed | tf_op | source)
XLA Modules:
  0.0 537.5 jit_solution(1263063015736483909)
XLA Ops:
  7.2 0.0 copy-start.1
  7.2 1.7 stack.2
  8.8 17.7 %all-to-all-start = ((bf16[16,128,128]{2,1,0:T(8,128)(2,1)}), bf16[16,128,128]{2,1,0:T(8,128)(2,1)S(1)}, u32[]{:S(2)}, u32[]{:S(2)}) async-start(bf16[16,128,128]{2,1,0:T(8,128)(2,1)} %stack.2), calls=%async_computation | async-start | bytes 1048576 | tf_op jit(solution)/shard_map/all_to_all | solution.py:18
  26.5 0.0 reduce-scatter.5.cloned.1.call-start
  26.5 48.7 %all_gather.3 = bf16[1024,128]{1,0:T(8,128)(2,1)S(1)} all-gather(bf16[32,128]{1,0:T(8,128)(2,1)} %param.8), channel_id=1, replica_groups=mesh['men'=32,'women'=16] {'men'}, dimensions={0}, use_global_device_ids=true | all-gather | bytes 270336 | tf_op jit(solution)/shard_map/all_gather | solution.py:20
  75.2 0.0 all-to-all-done
  75.2 0.0 copy-start.3
  75.2 0.0 copy-start.4
  75.2 4.8 multiply_reduce_fusion.2
  80.1 61.4 %psum.21 = f32[2048]{0:T(1024)S(1)} all-reduce(f32[2048]{0:T(1024)S(1)} %get-tuple-element.2), channel_id=1, replica_groups=mesh['men'=32,'women'=16] {'women'}, use_global_device_ids=true, to_apply=%region_1.0 | all-reduce | flops 2048 | bytes 16384 | tf_op jit(solution)/shard_map/psum | solution.py:36
  141.5 0.0 copy-done.1
  141.5 0.0 copy-start.2
  141.5 0.0 copy-start
  141.6 4.0 multiply_reduce_fusion
  145.6 60.7 %psum.22 = f32[1024]{0:T(1024)S(1)} all-reduce(f32[1024]{0:T(1024)S(1)} %multiply_reduce_fusion), channel_id=1, replica_groups=mesh['men'=32,'women'=16] {'men'}, use_global_device_ids=true, to_apply=%region_3.0 | all-reduce | flops 1024 | bytes 8192 | tf_op jit(solution)/shard_map/psum | solution.py:44
  206.3 0.0 copy-done.3
  206.3 0.0 copy-done.4
  206.3 4.0 multiply_reduce_fusion.1
  210.3 46.8 %psum.23 = f32[2048]{0:T(1024)S(1)} all-reduce(f32[2048]{0:T(1024)S(1)} %multiply_reduce_fusion.1), channel_id=1, replica_groups=mesh['men'=32,'women'=16] {'women'}, use_global_device_ids=true, to_apply=%region_5.0 | all-reduce | flops 2048 | bytes 16384 | tf_op jit(solution)/shard_map/psum | solution.py:56
  257.1 0.0 copy-done.2
  257.1 0.0 copy-done
  257.1 5.9 %fusion.4 = f32[1024,128]{1,0:T(8,128)} fusion(bf16[2048,128]{1,0:T(8,128)(2,1)S(1)} %bitcast.7, f32[2048,1024]{0,1:T(8,128)} %get-tuple-element.3, f32[2048]{0:T(1024)S(1)} %negate_divide_fusion, f32[1024]{0:T(1024)S(1)} %rsqrt_multiply_fusion, f32[2048]{0:T(1024)S(1)} %add_divide_fusion, f32[1024]{0:T(1024)S(1)} %copy-done), kind=kOutput, calls=%fused_computation.11 | convolution fusion | flops 549453824 | bytes 9461760 | tf_op jit(solution)/shard_map/dot_general | solution.py:70
  263.0 0.0 reduce-scatter.5.cloned.1.call-update
  263.0 0.0 reduce-scatter.3.cloned.1.call-start
  263.1 5.0 fusion.5
  268.1 6.1 %fusion.8 = f32[2048,128]{1,0:T(8,128)} fusion(f32[2048,128]{1,0:T(8,128)S(1)} %fusion.5, bf16[1024,128]{1,0:T(8,128)(2,1)S(1)} %all_gather.3, f32[2048,1024]{0,1:T(8,128)} %get-tuple-element.3, f32[1024]{0:T(1024)S(1)} %copy-done, f32[2048]{0:T(1024)S(1)} %negate_divide_fusion), kind=kOutput, calls=%fused_computation.15 | convolution fusion | flops 541851648 | bytes 10760192 | tf_op jit(solution)/shard_map/dot_general | solution.py:30
  274.1 0.0 reduce-scatter.3.cloned.1.call-update
  274.2 134.7 %reduce-scatter.5.cloned.1.call-done = f32[32,128]{1,0:T(8,128)} async-done(((f32[1024,128]{1,0:T(8,128)}), f32[32,128]{1,0:T(8,128)}) %reduce-scatter.5.cloned.1.call-update) | async-done | bytes 16400 | tf_op jit(solution)/shard_map/reduce_scatter | solution.py:77
  408.9 121.7 %reduce-scatter.3.cloned.1.call-done = f32[128,128]{1,0:T(8,128)} async-done(((f32[2048,128]{1,0:T(8,128)}), f32[128,128]{1,0:T(8,128)}) %reduce-scatter.3.cloned.1.call-update) | async-done | bytes 65552 | tf_op jit(solution)/shard_map/reduce_scatter | solution.py:59
  (3 shorter events, 0.0 us)
Async XLA Ops:
  7.2 134.3 %copy-start.1 = (s32[2048]{0:T(1024)S(1)}, s32[2048]{0:T(1024)}, u32[]{:S(2)}) copy-start(s32[2048]{0:T(1024)} %param.9) | copy-start | bytes 24580
  8.8 66.4 %all-to-all-start = ((bf16[16,128,128]{2,1,0:T(8,128)(2,1)}), bf16[16,128,128]{2,1,0:T(8,128)(2,1)S(1)}, u32[]{:S(2)}, u32[]{:S(2)}) async-start(bf16[16,128,128]{2,1,0:T(8,128)(2,1)} %stack.2), calls=%async_computation | async-start | bytes 1048576 | tf_op jit(solution)/shard_map/all_to_all | solution.py:18
  26.5 382.4 %reduce-scatter.5.cloned.1.call-start = ((), (), s32[]{:S(2)}) async-start(), calls=%async_computation.4 | async-start | bytes 540672 | tf_op jit(solution)/shard_map/reduce_scatter | solution.py:77
  75.2 131.1 %copy-start.3 = (s32[1024]{0:T(1024)S(1)}, s32[1024]{0:T(1024)}, u32[]{:S(2)}) copy-start(s32[1024]{0:T(1024)} %param.10) | copy-start | bytes 12292
  75.2 131.1 %copy-start.4 = (f32[1024]{0:T(1024)S(1)}, f32[1024]{0:T(1024)}, u32[]{:S(2)}) copy-start(f32[1024]{0:T(1024)} %param.13) | copy-start | bytes 12292
  141.5 115.6 %copy-start.2 = (f32[2048]{0:T(1024)S(1)}, f32[2048]{0:T(1024)}, u32[]{:S(2)}) copy-start(f32[2048]{0:T(1024)} %param.12) | copy-start | bytes 24580
  141.5 115.6 %copy-start = (f32[1024]{0:T(1024)S(1)}, f32[1024]{0:T(1024)}, u32[]{:S(2)}) copy-start(f32[1024]{0:T(1024)} %param.11) | copy-start | bytes 12292
  263.0 267.6 %reduce-scatter.3.cloned.1.call-start = ((), (), s32[]{:S(2)}) async-start(), calls=%async_computation.3 | async-start | bytes 1114112 | tf_op jit(solution)/shard_map/reduce_scatter | solution.py:59
Sparse Core Ops, SparseCore 0:
  263.2 145.6 reduce-scatter.4
  413.5 117.0 reduce-scatter.2

commit v2 on v0

--- a/solution.py
+++ b/solution.py
@@ -31,7 +31,7 @@
         return ((jnp.sum(weighted, axis=1), product), ())
 
     row_partial, weighted_v = sweep(first_work)[0]
-    row_mass = lax.psum(row_partial, "women")
+    row_mass = jnp.sum(lax.all_gather(row_partial, "women"), axis=0)
     men_disc = jnp.sqrt(row_mass * row_mass + 4.0 * men_mass)
     men_root = 2.0 * men_mass / (row_mass + men_disc)
 

time: 562 us -> 561 us (level)
    psum x1 -> x0, blocking collectives: 46.7 us -> none  [body(): row_mass = lax.psum(row_partial, 'women')]
    all_gather x0 -> x1, blocking collectives: none -> 45.9 us  [body(): row_mass = jnp.sum(lax.all_gather(row_partial, 'women'), axis=0)]
where the time goes in v2:
time: 561 us
  blocking collectives  262 us (47%)
  waiting for transfers between devices  254 us (45%)
  matrix products  21.7 us (4%)
  between operations  14.1 us (3%)
  other arithmetic  8.08 us (1%)
    reduce_scatter x1, waiting for transfers between devices, body(): lax.psum_scatter(women_terms, 'men', scatter_dimension=0, tiled=True)  133 us
    reduce_scatter x1, waiting for transfers between devices, body(): lax.psum_scatter(men_term, 'women', scatter_dimension=0, tiled=True)  122 us
    psum x1, blocking collectives, body(): col_mass = lax.psum(col_partial, 'men')  64.6 us
    all_gather x1, blocking collectives, body(): men_rows = lax.all_gather(men_embed, 'women', axis=0, tiled=True)  58.4 us
    psum x1, blocking collectives, body(): row_cot = lax.psum(row_back, 'women')  48.8 us
    all_gather x1, blocking collectives, body(): row_mass = jnp.sum(lax.all_gather(row_partial, 'women'), axis=0)  45.9 us
    all_gather x1, blocking collectives, body(): women_rows = lax.all_gather(women_embed, 'men', axis=0, tiled=True)  44.3 us
  transfers between devices with their start and end apart: 2, of which 2 were waited for; matrix products, arithmetic and copies ran while one was open for 2% of the time, Pallas kernels for 0%

profile of v2, /device:TPU:8, one launch (start us, length us, event | category | flops | bytes accessed | tf_op | source)
XLA Modules:
  0.0 560.5 jit_solution(6000826547724597634)
XLA Ops:
  7.2 0.0 copy-start.1
  7.2 0.0 reduce-scatter.5.cloned.1.call-start
  7.2 44.3 %all_gather.13 = bf16[1024,128]{1,0:T(8,128)(2,1)S(1)} all-gather(bf16[32,128]{1,0:T(8,128)(2,1)} %param.8), channel_id=1, replica_groups=mesh['men'=32,'women'=16] {'men'}, dimensions={0}, use_global_device_ids=true | all-gather | bytes 270336 | tf_op jit(solution)/shard_map/all_gather | solution.py:18
  51.5 58.4 %all_gather.12 = bf16[2048,128]{1,0:T(8,128)(2,1)S(1)} all-gather(bf16[128,128]{1,0:T(8,128)(2,1)} %param.7), channel_id=1, replica_groups=mesh['men'=32,'women'=16] {'women'}, dimensions={0}, use_global_device_ids=true | all-gather | bytes 557056 | tf_op jit(solution)/shard_map/all_gather | solution.py:17
  109.9 0.0 copy-start.3
  109.9 0.0 copy-start.4
  109.9 4.8 multiply_reduce_fusion.2
  114.7 45.9 %all-gather = f32[32768]{0:T(1024)S(1)} all-gather(f32[2048]{0:T(1024)S(1)} %get-tuple-element.2), channel_id=2, replica_groups=mesh['men'=32,'women'=16] {'women'}, dimensions={0}, use_global_device_ids=true | all-gather | bytes 139264 | tf_op jit(solution)/shard_map/all_gather | solution.py:34
  160.7 0.0 copy-done.1
  160.7 0.0 copy-start.2
  160.7 0.0 copy-start
  160.7 4.0 multiply_reduce_fusion
  164.7 64.6 %psum.14 = f32[1024]{0:T(1024)S(1)} all-reduce(f32[1024]{0:T(1024)S(1)} %multiply_reduce_fusion), channel_id=1, replica_groups=mesh['men'=32,'women'=16] {'men'}, use_global_device_ids=true, to_apply=%region_3.0 | all-reduce | flops 1024 | bytes 8192 | tf_op jit(solution)/shard_map/psum | solution.py:42
  229.3 0.0 copy-done.3
  229.3 0.0 copy-done.4
  229.4 4.0 multiply_reduce_fusion.1
  233.4 48.8 %psum.15 = f32[2048]{0:T(1024)S(1)} all-reduce(f32[2048]{0:T(1024)S(1)} %multiply_reduce_fusion.1), channel_id=1, replica_groups=mesh['men'=32,'women'=16] {'women'}, use_global_device_ids=true, to_apply=%region_5.0 | all-reduce | flops 2048 | bytes 16384 | tf_op jit(solution)/shard_map/psum | solution.py:54
  282.2 0.0 copy-done.2
  282.2 0.0 copy-done
  282.2 5.9 %fusion.4 = f32[1024,128]{1,0:T(8,128)} fusion(bf16[2048,128]{1,0:T(8,128)(2,1)S(1)} %all_gather.12, f32[2048,1024]{0,1:T(8,128)} %get-tuple-element.3, f32[2048]{0:T(1024)S(1)} %negate_divide_fusion, f32[1024]{0:T(1024)S(1)} %rsqrt_multiply_fusion, f32[2048]{0:T(1024)S(1)} %add_divide_fusion, f32[1024]{0:T(1024)S(1)} %copy-done), kind=kOutput, calls=%fused_computation.11 | convolution fusion | flops 549453824 | bytes 9461760 | tf_op jit(solution)/shard_map/dot_general | solution.py:68
  288.1 0.0 reduce-scatter.5.cloned.1.call-update
  288.1 0.0 reduce-scatter.3.cloned.1.call-start
  288.2 5.0 fusion.5
  293.2 6.1 %fusion.8 = f32[2048,128]{1,0:T(8,128)} fusion(f32[2048,128]{1,0:T(8,128)S(1)} %fusion.5, bf16[1024,128]{1,0:T(8,128)(2,1)S(1)} %all_gather.13, f32[2048,1024]{0,1:T(8,128)} %get-tuple-element.3, f32[1024]{0:T(1024)S(1)} %copy-done, f32[2048]{0:T(1024)S(1)} %negate_divide_fusion), kind=kOutput, calls=%fused_computation.15 | convolution fusion | flops 541851648 | bytes 10760192 | tf_op jit(solution)/shard_map/dot_general | solution.py:28
  299.2 0.0 reduce-scatter.3.cloned.1.call-update
  299.2 132.7 %reduce-scatter.5.cloned.1.call-done = f32[32,128]{1,0:T(8,128)} async-done(((f32[1024,128]{1,0:T(8,128)}), f32[32,128]{1,0:T(8,128)}) %reduce-scatter.5.cloned.1.call-update) | async-done | bytes 16400 | tf_op jit(solution)/shard_map/reduce_scatter | solution.py:75
  432.0 121.7 %reduce-scatter.3.cloned.1.call-done = f32[128,128]{1,0:T(8,128)} async-done(((f32[2048,128]{1,0:T(8,128)}), f32[128,128]{1,0:T(8,128)}) %reduce-scatter.3.cloned.1.call-update) | async-done | bytes 65552 | tf_op jit(solution)/shard_map/reduce_scatter | solution.py:57
  (5 shorter events, 0.1 us)
Async XLA Ops:
  7.2 153.5 %copy-start.1 = (s32[2048]{0:T(1024)S(1)}, s32[2048]{0:T(1024)}, u32[]{:S(2)}) copy-start(s32[2048]{0:T(1024)} %param.9) | copy-start | bytes 24580
  7.2 424.8 %reduce-scatter.5.cloned.1.call-start = ((), (), s32[]{:S(2)}) async-start(), calls=%async_computation.3 | async-start | bytes 540672 | tf_op jit(solution)/shard_map/reduce_scatter | solution.py:75
  109.9 119.4 %copy-start.3 = (s32[1024]{0:T(1024)S(1)}, s32[1024]{0:T(1024)}, u32[]{:S(2)}) copy-start(s32[1024]{0:T(1024)} %param.10) | copy-start | bytes 12292
  109.9 119.4 %copy-start.4 = (f32[1024]{0:T(1024)S(1)}, f32[1024]{0:T(1024)}, u32[]{:S(2)}) copy-start(f32[1024]{0:T(1024)} %param.13) | copy-start | bytes 12292
  160.7 121.5 %copy-start.2 = (f32[2048]{0:T(1024)S(1)}, f32[2048]{0:T(1024)}, u32[]{:S(2)}) copy-start(f32[2048]{0:T(1024)} %param.12) | copy-start | bytes 24580
  160.7 121.5 %copy-start = (f32[1024]{0:T(1024)S(1)}, f32[1024]{0:T(1024)}, u32[]{:S(2)}) copy-start(f32[1024]{0:T(1024)} %param.11) | copy-start | bytes 12292
  288.1 265.6 %reduce-scatter.3.cloned.1.call-start = ((), (), s32[]{:S(2)}) async-start(), calls=%async_computation.2 | async-start | bytes 1114112 | tf_op jit(solution)/shard_map/reduce_scatter | solution.py:57
Sparse Core Ops, SparseCore 0:
  288.2 143.6 reduce-scatter.4
  436.6 117.0 reduce-scatter.2
